TPU v7x, 32 devices: a whole 2x2x4 slice. The times are simulated.
32 devices in a mesh: dp: 8 (over y, x, core), mp: 4 (over z).
Axes of the slice: x: 2, y: 2, z: 4, core: 2. Of those that a mesh axis runs over, the one named last changes fastest.
Arguments:
- activations: bfloat16 [4, 16, 1024, 4096], P(None, 'dp', 'mp'), may hold values from -6 to 6
- cotangents: bfloat16 [4, 16, 1024, 4096], P(None, 'dp', 'mp'), may hold values from -0.1875 to 0.1875
- lengths: int32 [16], P('dp'), may hold values from 128 to 1024, as said below
- project_in: bfloat16 [4, 64, 4096], replicated, may hold values from -0.09375 to 0.09375
- project_out: bfloat16 [4, 64, 4096], replicated, may hold values from -0.09375 to 0.09375
- preconditioner: bfloat16 [16384, 4096], P('mp', 'dp'), as said below
- queries: bfloat16 [8192, 16384], P('dp', 'mp'), may hold values from -0.0625 to 0.0625
Outputs:
- scores: float32 [16, 8192], P(None, ('dp', 'mp'))
Inputs may be any that keep to these rules, and one draw needn't show every extreme that they name: `lengths`: positions at or past an example's length are padding; some example has all 1024 positions live. `preconditioner`: each layer's 4096 x 4096 block is symmetric.
All inputs are finite; a program needn't handle non-finite values.
Results may differ from a plain program's by a relative error of at most 0.005.
Values may be sent and summed in bfloat16 or wider, within the bound.
No kernel may reach another device: no remote copies, remote signals or barrier semaphores. Data moves between devices by JAX's collectives and lax.ppermute only.
A program may use at most 128 MiB of HBM per device.

v0:
```python
import jax
import jax.numpy as jnp
from jax import lax
from jax.sharding import PartitionSpec as P


def split_parts(dense):
    upper = dense.astype(jnp.bfloat16)
    kept = lax.optimization_barrier(upper)
    lower = (dense - kept.astype(jnp.float32)).astype(jnp.bfloat16)
    return (upper, lower)


def body(activations, cotangents, lengths, project_in, project_out, preconditioner, queries):
    width_mp = lax.axis_size("mp")
    layer_count = activations.shape[0]
    tokens_here = activations.shape[2]
    factor_size = project_in.shape[1]
    block_size = factor_size * factor_size
    group_size = width_mp // layer_count
    mp_place = lax.axis_index("mp")
    contract = (((1,), (1,)), ((), ()))
    positions = mp_place * tokens_here + jnp.arange(tokens_here, dtype=jnp.int32)
    live_mask = positions[None, :] < lengths[:, None]
    left_factor = jnp.einsum(
        "lesd,lkd->lesk", activations, project_in, preferred_element_type=jnp.float32
    ).astype(jnp.bfloat16)
    right_factor = jnp.einsum(
        "lesd,lkd->lesk", cotangents, project_out, preferred_element_type=jnp.float32
    )
    right_factor = jnp.where(live_mask[None, :, :, None], right_factor, 0.0).astype(jnp.bfloat16)
    partial_grad = jnp.einsum(
        "lesj,lesc->eljc", right_factor, left_factor, preferred_element_type=jnp.float32
    )
    partial_grad = partial_grad.reshape(partial_grad.shape[0], layer_count * block_size)
    grad_total = lax.psum(partial_grad, "mp")
    layer_place = mp_place // group_size
    grad_layer = lax.dynamic_slice_in_dim(
        grad_total, layer_place * block_size, block_size, 1
    ).astype(jnp.bfloat16)
    spread = lax.all_to_all(grad_layer, "dp", split_axis=1, concat_axis=0, tiled=True)
    partial_pre = lax.dot_general(
        spread, preconditioner, contract, preferred_element_type=jnp.float32
    )
    precond_grad = lax.psum(partial_pre, "dp")
    upper_grad, lower_grad = split_parts(precond_grad)
    scores = lax.psum_scatter(
        lax.dot_general(queries, upper_grad, contract, preferred_element_type=jnp.float32)
        + lax.dot_general(queries, lower_grad, contract, preferred_element_type=jnp.float32),
        "mp",
        scatter_dimension=0,
        tiled=True,
    )
    return scores.T


def solution(mesh):
    return jax.shard_map(
        body,
        mesh=mesh,
        in_specs=(
            P(None, "dp", "mp", None),
            P(None, "dp", "mp", None),
            P("dp"),
            P(),
            P(),
            P("mp", "dp"),
            P("dp", "mp"),
        ),
        out_specs=P(None, ("dp", "mp")),
        check_vma=False,
    )
```

profile of v0, /device:TPU:0, one launch (start us, length us, event | category | flops | bytes accessed | tf_op | source)
XLA Modules:
  0.0 151.0 jit_solution(13580495785346025847)
XLA Ops:
  6.5 0.0 copy-start
  6.5 0.0 all-reduce.3.cloned.1.call-start
  6.5 0.9 broadcast_compare_fusion
  7.4 0.7 copy-done
  8.1 8.8 %fusion.16 = bf16[4,2,256,64]{2,3,0,1:T(8,128)(2,1)S(1)} fusion(bf16[4,64,4096]{2,1,0:T(8,128)(2,1)S(1)} %copy-done, bf16[4,2,256,4096]{3,2,1,0:T(8,128)(2,1)} %param.8, pred[2,256]{1,0:T(4,128)(4,1)S(1)} %broadcast_compare_fusion), kind=kOutput, calls=%fused_computation.8 | convolution fusion | flops 1074003968 | bytes 19137024 | tf_op jit(solution)/shard_map/lesd,lkd->lesk/dot_general | solution.py:28
  16.9 9.3 %fusion.24 = f32[2,4,64,64]{3,2,1,0:T(8,128)S(1)} fusion(bf16[4,2,256,64]{2,3,0,1:T(8,128)(2,1)S(1)} %fusion.16, bf16[4,64,4096]{2,1,0:T(8,128)(2,1)} %param.10, bf16[4,2,256,4096]{3,2,1,0:T(8,128)(2,1)} %param.7), kind=kOutput, calls=%fused_computation.11 | convolution fusion | flops 1090650112 | bytes 19267584 | tf_op jit(solution)/shard_map/lesj,lesc->eljc/dot_general | solution.py:32
  26.2 0.1 reshape.40
  26.3 23.0 %all-reduce.4 = bf16[2,16384]{1,0:T(2,128)(2,1)S(1)} all-reduce(f32[2,16384]{1,0:T(2,128)S(1)} %reshape.40), channel_id=1, replica_groups=mesh['dp'=8,'mp'=4] {'mp'}, use_global_device_ids=true, to_apply=%region_0.1 | all-reduce | flops 32768 | bytes 196608 | tf_op jit(solution)/shard_map/psum | solution.py:36
  49.4 8.3 %all_to_all.19 = bf16[2,8,512]{2,0,1:T(2,128)(2,1)S(1)} all-to-all(bf16[2,8,512]{2,0,1:T(2,128)(2,1)S(1)} %bitcast.27), channel_id=1, replica_groups=mesh['dp'=8,'mp'=4] {'dp'}, dimensions={1} | all-to-all | bytes 32768 | tf_op jit(solution)/shard_map/all_to_all | solution.py:41
  57.7 4.1 %fusion.27 = f32[16,4096]{1,0:T(8,128)} fusion(bf16[16,512]{1,0:T(8,128)(2,1)S(1)} %all_to_all.17, bf16[4096,512]{1,0:T(8,128)(2,1)} %param.12), kind=kOutput, calls=%fused_computation.16 | convolution fusion | flops 67108864 | bytes 4472832 | tf_op jit(solution)/shard_map/dot_general | solution.py:42
  61.7 0.0 all-reduce.3.cloned.1.call-update
  61.8 0.0 reduce-scatter.2.cloned.1.call-start
  61.8 50.5 %all-reduce.3.cloned.1.call-done = f32[16,4096]{1,0:T(8,128)} async-done(((f32[16,4096]{1,0:T(8,128)}), f32[16,4096]{1,0:T(8,128)}) %all-reduce.3.cloned.1.call-update) | async-done | bytes 262160 | tf_op jit(solution)/shard_map/psum | solution.py:45
  112.3 0.0 copy-start.1
  112.3 1.0 convert_element_type.21
  113.3 5.6 %fusion.28 = f32[16,1024]{1,0:T(8,128)S(1)} fusion(bf16[16,4096]{1,0:T(8,128)(2,1)S(1)} %convert_element_type.21, bf16[1024,4096]{1,0:T(8,128)(2,1)} %param.13), kind=kOutput, calls=%fused_computation.17 | convolution fusion | flops 134217728 | bytes 8585216 | tf_op jit(solution)/shard_map/dot_general | solution.py:48
  119.0 0.0 copy-done.1
  119.0 6.3 %fusion.21 = f32[1024,16]{0,1:T(8,128)} fusion(f32[16,1024]{1,0:T(8,128)S(1)} %fusion.28, bf16[1024,4096]{1,0:T(8,128)(2,1)} %param.13, f32[16,4096]{1,0:T(8,128)S(1)} %copy-done.1, bf16[16,4096]{1,0:T(8,128)(2,1)S(1)} %convert_element_type.21), kind=kOutput, calls=%fused_computation.10 | convolution fusion | flops 134430720 | bytes 8912896 | tf_op jit(solution)/shard_map/dot_general | solution.py:49
  125.3 0.0 reduce-scatter.2.cloned.1.call-update
  125.3 18.9 %reduce-scatter.2.cloned.1.call-done = f32[256,16]{0,1:T(8,128)} async-done(((f32[1024,16]{0,1:T(8,128)}), f32[256,16]{0,1:T(8,128)}) %reduce-scatter.2.cloned.1.call-update) | async-done | bytes 16400 | tf_op jit(solution)/shard_map/reduce_scatter | solution.py:47
  (3 shorter events, 0.0 us)
Async XLA Ops:
  6.5 1.6 %copy-start = (bf16[4,64,4096]{2,1,0:T(8,128)(2,1)S(1)}, bf16[4,64,4096]{2,1,0:T(8,128)(2,1)}, u32[]{:S(2)}) copy-start(bf16[4,64,4096]{2,1,0:T(8,128)(2,1)} %param.11) | copy-start | bytes 6291460
  6.5 105.8 %all-reduce.3.cloned.1.call-start = ((), (), s32[]{:S(2)}) async-start(), calls=%async_computation.2 | async-start | bytes 524288 | tf_op jit(solution)/shard_map/psum | solution.py:45
  61.8 82.4 %reduce-scatter.2.cloned.1.call-start = ((), (), s32[]{:S(2)}) async-start(), calls=%async_computation.3 | async-start | bytes 81920 | tf_op jit(solution)/shard_map/reduce_scatter | solution.py:47
  112.3 6.7 %copy-start.1 = (f32[16,4096]{1,0:T(8,128)S(1)}, f32[16,4096]{1,0:T(8,128)}, u32[]{:S(2)}) copy-start(f32[16,4096]{1,0:T(8,128)} %all-reduce.3.cloned.1.call-done) | copy-start | bytes 786436
Sparse Core Ops, SparseCore 0:
  61.9 50.3 all-reduce.2
  125.4 18.6 reduce-scatter.1
where the time goes:
time: 151 us
  waiting for transfers between devices  69.4 us (46%)
  matrix products  34.1 us (23%)
  blocking collectives  31.3 us (21%)
  between operations  13.4 us (9%)
  other arithmetic  1.91 us (1%)
    psum x1, waiting for transfers between devices, body(): precond_grad = lax.psum(partial_pre, 'dp')  50.5 us
    psum x1, blocking collectives, body(): grad_total = lax.psum(partial_grad, 'mp')  23 us
    reduce_scatter x1, waiting for transfers between devices, body(): lax.psum_scatter(lax.dot_general(queries, upper_grad, contract, preferred...  18.9 us
    dot_general x1, matrix products, body(): jnp.einsum('lesj,lesc->eljc', right_factor, left_factor, preferred_elemen...  9.26 us
    dot_general x1, matrix products, body(): jnp.einsum('lesd,lkd->lesk', cotangents, project_out, preferred_element_t...  8.75 us
    all_to_all x1, blocking collectives, body(): lax.all_to_all(grad_layer, 'dp', split_axis=1, concat_axis=0, tiled=True)  8.27 us
    dot_general x1, matrix products, body(): lax.dot_general(queries, lower_grad, contract, preferred_element_type=jnp...  6.3 us
    dot_general x1, matrix products, body(): lax.dot_general(queries, upper_grad, contract, preferred_element_type=jnp...  5.65 us
  transfers between devices with their start and end apart: 2, of which 2 were waited for; matrix products, arithmetic and copies ran while one was open for 0% of the time, Pallas kernels for 0%

commit v1 on v0

--- a/solution.py
+++ b/solution.py
@@ -33,7 +33,11 @@
         "lesj,lesc->eljc", right_factor, left_factor, preferred_element_type=jnp.float32
     )
     partial_grad = partial_grad.reshape(partial_grad.shape[0], layer_count * block_size)
-    grad_total = lax.psum(partial_grad, "mp")
+    grad_total = partial_grad
+    for hop in (1, 2):
+        grad_total = grad_total + lax.ppermute(
+            grad_total, "mp", [(dev, dev ^ hop) for dev in range(4)]
+        )
     layer_place = mp_place // group_size
     grad_layer = lax.dynamic_slice_in_dim(
         grad_total, layer_place * block_size, block_size, 1

time: 151 us -> 146 us (0.967)
  blocking collectives: 31.3 us -> 8.17 us
  waiting for transfers between devices: 69.4 us -> 81.2 us
  starting transfers between devices: 0.04 us -> 5.98 us
    psum x1 -> x0, blocking collectives: 23 us -> none  [body(): grad_total = lax.psum(partial_grad, 'mp')]
    ppermute x0 -> x2, waiting for transfers between devices: none -> 9.1 us  [body(): lax.ppermute(grad_total, 'mp', [(dev, dev ^ hop) for dev in range(4)])]
    ppermute x0 -> x2, starting transfers between devices: none -> 5.94 us  [body(): lax.ppermute(grad_total, 'mp', [(dev, dev ^ hop) for dev in range(4)])]
    psum x1, waiting for transfers between devices: 50.5 us -> 53.2 us  [body(): precond_grad = lax.psum(partial_pre, 'dp')]
  transfers between devices with their start and end apart: 2 -> 4, of which waited for: 2 -> 4; matrix products, arithmetic and copies ran while one was open for 0% -> 0% of each run, Pallas kernels for 0% -> 0%
where the time goes in v1:
time: 146 us
  waiting for transfers between devices  81.2 us (56%)
  matrix products  34.1 us (23%)
  between operations  13.4 us (9%)
  blocking collectives  8.17 us (6%)
  starting transfers between devices  5.98 us (4%)
  other arithmetic  2 us (1%)
    psum x1, waiting for transfers between devices, body(): precond_grad = lax.psum(partial_pre, 'dp')  53.2 us
    reduce_scatter x1, waiting for transfers between devices, body(): lax.psum_scatter(lax.dot_general(queries, upper_grad, contract, preferred...  18.9 us
    dot_general x1, matrix products, body(): jnp.einsum('lesj,lesc->eljc', right_factor, left_factor, preferred_elemen...  9.26 us
    ppermute x2, waiting for transfers between devices, body(): lax.ppermute(grad_total, 'mp', [(dev, dev ^ hop) for dev in range(4)])  9.1 us
    dot_general x1, matrix products, body(): jnp.einsum('lesd,lkd->lesk', cotangents, project_out, preferred_element_t...  8.75 us
    all_to_all x1, blocking collectives, body(): lax.all_to_all(grad_layer, 'dp', split_axis=1, concat_axis=0, tiled=True)  8.17 us
    dot_general x1, matrix products, body(): lax.dot_general(queries, lower_grad, contract, preferred_element_type=jnp...  6.3 us
    ppermute x2, starting transfers between devices, body(): lax.ppermute(grad_total, 'mp', [(dev, dev ^ hop) for dev in range(4)])  5.94 us
  transfers between devices with their start and end apart: 4, of which 4 were waited for; matrix products, arithmetic and copies ran while one was open for 0% of the time, Pallas kernels for 0%

profile of v1, /device:TPU:0, one launch (start us, length us, event | category | flops | bytes accessed | tf_op | source)
XLA Modules:
  0.0 145.7 jit_solution(3145897021451915246)
XLA Ops:
  6.5 0.0 copy-start
  6.5 0.0 all-reduce.2.cloned.1.call-start
  6.5 0.9 broadcast_compare_fusion
  7.4 0.7 copy-done
  8.1 8.8 %fusion.16 = bf16[4,2,256,64]{2,3,0,1:T(8,128)(2,1)S(1)} fusion(bf16[4,64,4096]{2,1,0:T(8,128)(2,1)S(1)} %copy-done, bf16[4,2,256,4096]{3,2,1,0:T(8,128)(2,1)} %param.8, pred[2,256]{1,0:T(4,128)(4,1)S(1)} %broadcast_compare_fusion), kind=kOutput, calls=%fused_computation.8 | convolution fusion | flops 1074003968 | bytes 19137024 | tf_op jit(solution)/shard_map/lesd,lkd->lesk/dot_general | solution.py:28
  16.9 9.3 %fusion.24 = f32[2,4,64,64]{3,2,1,0:T(8,128)S(1)} fusion(bf16[4,2,256,64]{2,3,0,1:T(8,128)(2,1)S(1)} %fusion.16, bf16[4,64,4096]{2,1,0:T(8,128)(2,1)} %param.10, bf16[4,2,256,4096]{3,2,1,0:T(8,128)(2,1)} %param.7), kind=kOutput, calls=%fused_computation.11 | convolution fusion | flops 1090650112 | bytes 19267584 | tf_op jit(solution)/shard_map/lesj,lesc->eljc/dot_general | solution.py:32
  26.2 0.1 reshape.40
  26.3 3.1 %collective-permute-start = (f32[2,16384]{1,0:T(2,128)S(1)}, f32[2,16384]{1,0:T(2,128)S(1)}, u32[]{:S(2)}, u32[]{:S(2)}) collective-permute-start(f32[2,16384]{1,0:T(2,128)S(1)} %reshape.40), channel_id=1, source_target_pairs={{0,1},{1,0},{2,3},{3,2},{4,5},{5,4},{6,7},{7,6},{8,9},{9,8},{10,11... | collective-permute-start | bytes 393224 | tf_op jit(solution)/shard_map/ppermute | solution.py:38
  29.4 3.5 %collective-permute-done = f32[2,16384]{1,0:T(2,128)S(1)} collective-permute-done((f32[2,16384]{1,0:T(2,128)S(1)}, f32[2,16384]{1,0:T(2,128)S(1)}, u32[]{:S(2)}, u32[]{:S(2)}) %collective-permute-start) | collective-permute-done | bytes 131104 | tf_op jit(solution)/shard_map/ppermute | solution.py:38
  32.9 0.1 add.32
  33.0 2.8 %collective-permute-start.1 = (f32[2,16384]{1,0:T(2,128)S(1)}, f32[2,16384]{1,0:T(2,128)S(1)}, u32[]{:S(2)}, u32[]{:S(2)}) collective-permute-start(f32[2,16384]{1,0:T(2,128)S(1)} %add.32), channel_id=1, source_target_pairs={{0,2},{1,3},{2,0},{3,1},{4,6},{5,7},{6,4},{7,5},{8,10},{9,11},{10,... | collective-permute-start | bytes 393224 | tf_op jit(solution)/shard_map/ppermute | solution.py:38
  35.8 5.6 %collective-permute-done.1 = f32[2,16384]{1,0:T(2,128)S(1)} collective-permute-done((f32[2,16384]{1,0:T(2,128)S(1)}, f32[2,16384]{1,0:T(2,128)S(1)}, u32[]{:S(2)}, u32[]{:S(2)}) %collective-permute-start.1) | collective-permute-done | bytes 131104 | tf_op jit(solution)/shard_map/ppermute | solution.py:38
  41.5 8.2 %all_to_all.19 = bf16[2,8,512]{2,0,1:T(2,128)(2,1)S(1)} all-to-all(bf16[2,8,512]{2,0,1:T(2,128)(2,1)S(1)} %bitcast.27), channel_id=1, replica_groups=mesh['dp'=8,'mp'=4] {'dp'}, dimensions={1} | all-to-all | bytes 32768 | tf_op jit(solution)/shard_map/all_to_all | solution.py:45
  49.6 4.1 %fusion.28 = f32[16,4096]{1,0:T(8,128)} fusion(bf16[16,512]{1,0:T(8,128)(2,1)S(1)} %all_to_all.17, bf16[4096,512]{1,0:T(8,128)(2,1)} %param.12), kind=kOutput, calls=%fused_computation.17 | convolution fusion | flops 67108864 | bytes 4472832 | tf_op jit(solution)/shard_map/dot_general | solution.py:46
  53.7 0.0 all-reduce.2.cloned.1.call-update
  53.8 0.0 reduce-scatter.2.cloned.1.call-start
  53.8 53.2 %all-reduce.2.cloned.1.call-done = f32[16,4096]{1,0:T(8,128)} async-done(((f32[16,4096]{1,0:T(8,128)}), f32[16,4096]{1,0:T(8,128)}) %all-reduce.2.cloned.1.call-update) | async-done | bytes 262160 | tf_op jit(solution)/shard_map/psum | solution.py:49
  107.0 0.0 copy-start.1
  107.0 1.0 convert_element_type.21
  108.1 5.6 %fusion.29 = f32[16,1024]{1,0:T(8,128)S(1)} fusion(bf16[16,4096]{1,0:T(8,128)(2,1)S(1)} %convert_element_type.21, bf16[1024,4096]{1,0:T(8,128)(2,1)} %param.13), kind=kOutput, calls=%fused_computation.18 | convolution fusion | flops 134217728 | bytes 8585216 | tf_op jit(solution)/shard_map/dot_general | solution.py:52
  113.7 0.0 copy-done.1
  113.7 6.3 %fusion.21 = f32[1024,16]{0,1:T(8,128)} fusion(f32[16,1024]{1,0:T(8,128)S(1)} %fusion.29, bf16[1024,4096]{1,0:T(8,128)(2,1)} %param.13, f32[16,4096]{1,0:T(8,128)S(1)} %copy-done.1, bf16[16,4096]{1,0:T(8,128)(2,1)S(1)} %convert_element_type.21), kind=kOutput, calls=%fused_computation.10 | convolution fusion | flops 134430720 | bytes 8912896 | tf_op jit(solution)/shard_map/dot_general | solution.py:53
  120.0 0.0 reduce-scatter.2.cloned.1.call-update
  120.0 18.9 %reduce-scatter.2.cloned.1.call-done = f32[256,16]{0,1:T(8,128)} async-done(((f32[1024,16]{0,1:T(8,128)}), f32[256,16]{0,1:T(8,128)}) %reduce-scatter.2.cloned.1.call-update) | async-done | bytes 16400 | tf_op jit(solution)/shard_map/reduce_scatter | solution.py:51
  (3 shorter events, 0.0 us)
Async XLA Ops:
  6.5 1.6 %copy-start = (bf16[4,64,4096]{2,1,0:T(8,128)(2,1)S(1)}, bf16[4,64,4096]{2,1,0:T(8,128)(2,1)}, u32[]{:S(2)}) copy-start(bf16[4,64,4096]{2,1,0:T(8,128)(2,1)} %param.11) | copy-start | bytes 6291460
  6.5 100.5 %all-reduce.2.cloned.1.call-start = ((), (), s32[]{:S(2)}) async-start(), calls=%async_computation.2 | async-start | bytes 524288 | tf_op jit(solution)/shard_map/psum | solution.py:49
  26.3 6.6 %collective-permute-start = (f32[2,16384]{1,0:T(2,128)S(1)}, f32[2,16384]{1,0:T(2,128)S(1)}, u32[]{:S(2)}, u32[]{:S(2)}) collective-permute-start(f32[2,16384]{1,0:T(2,128)S(1)} %reshape.40), channel_id=1, source_target_pairs={{0,1},{1,0},{2,3},{3,2},{4,5},{5,4},{6,7},{7,6},{8,9},{9,8},{10,11... | collective-permute-start | bytes 393224 | tf_op jit(solution)/shard_map/ppermute | solution.py:38
  33.0 8.4 %collective-permute-start.1 = (f32[2,16384]{1,0:T(2,128)S(1)}, f32[2,16384]{1,0:T(2,128)S(1)}, u32[]{:S(2)}, u32[]{:S(2)}) collective-permute-start(f32[2,16384]{1,0:T(2,128)S(1)} %add.32), channel_id=1, source_target_pairs={{0,2},{1,3},{2,0},{3,1},{4,6},{5,7},{6,4},{7,5},{8,10},{9,11},{10,... | collective-permute-start | bytes 393224 | tf_op jit(solution)/shard_map/ppermute | solution.py:38
  53.8 85.1 %reduce-scatter.2.cloned.1.call-start = ((), (), s32[]{:S(2)}) async-start(), calls=%async_computation.3 | async-start | bytes 81920 | tf_op jit(solution)/shard_map/reduce_scatter | solution.py:51
  107.0 6.7 %copy-start.1 = (f32[16,4096]{1,0:T(8,128)S(1)}, f32[16,4096]{1,0:T(8,128)}, u32[]{:S(2)}) copy-start(f32[16,4096]{1,0:T(8,128)} %all-reduce.2.cloned.1.call-done) | copy-start | bytes 786436
Sparse Core Ops, SparseCore 0:
  53.9 53.0 all-reduce.1
  120.2 18.6 reduce-scatter.1
